TPU v7x, 256 devices: a whole 4x4x8 slice. The times are simulated.
256 devices in a mesh: samp: 64 (over x, z, core), blk: 4 (over y).
Axes of the slice: x: 4, y: 4, z: 8, core: 2. Of those that a mesh axis runs over, the one named last changes fastest.
Arguments:
- dosages: bfloat16 [40960, 2048], P('samp', 'blk'), may hold values from 0 to 2
- traits: bfloat16 [16, 40960], P(None, 'samp'), may hold values from -6 to 6
- folds: int32 [40960], P('samp'), may hold values from 0 to 4
Outputs:
- level0: float32 [4, 5, 16, 40960], P(None, None, 'blk', 'samp')
- blend: float32 [16, 40960], P('blk', 'samp')
All inputs are finite; a program needn't handle non-finite values.
Results may differ from a plain program's by a relative error of at most 0.0097.
Values may be sent and summed in bfloat16 or wider, within the bound.
No kernel may reach another device: no remote copies, remote signals or barrier semaphores. Data moves between devices by JAX's collectives and lax.ppermute only.
A program may use at most 64 MiB of HBM per device.

v0:
```python
import jax
import jax.numpy as jnp
import numpy as np
from jax import lax
from jax.sharding import Mesh
from jax.sharding import PartitionSpec as P

FOLDS = 5
SHRINK = 5
RATIOS = (99.0, 3.0, 1.0, 1.0 / 3.0, 1.0 / 99.0)
EPS = 1e-05
HIGH = lax.Precision.HIGHEST
SAMP = ("x", "z", "c")


def solve_batch(systems, right_sides):
    factors = jnp.linalg.cholesky(systems)

    def solve_single(factor, right_side):
        return jax.scipy.linalg.cho_solve((factor, True), right_side)

    return jax.vmap(solve_single)(factors, right_sides)


def psum_tree(value):
    for name in ("c", "z", "x"):
        value = lax.psum(value, name)
    return value


def shards(dosages, traits, folds):
    rows, width = dosages.shape
    traits_count = traits.shape[0]
    fold_ids = jnp.arange(FOLDS, dtype=jnp.int32)
    masks = (folds[None, :] == fold_ids[:, None]).astype(jnp.float32)
    mask_half = masks.astype(jnp.bfloat16)
    traits_wide = traits.astype(jnp.float32)
    augmented = jnp.concatenate([dosages, jnp.ones((rows, 1), jnp.bfloat16), traits.T], axis=1)
    weighted = mask_half[:, :, None] * augmented[None]
    stats = jnp.einsum("ri,krj->kij", augmented, weighted, preferred_element_type=jnp.float32)
    stats = lax.psum(stats, SAMP)
    gram = stats[:, :width, :width]
    sums = stats[:, :width, width]
    counts = stats[:, width, width]
    cross = stats[:, width + 1 :, :width]
    trait_sums = stats[:, width + 1 :, width]
    total = jnp.sum(counts)
    mean = jnp.sum(sums, axis=0) / total
    gram_total = jnp.sum(gram, axis=0)
    variance = jnp.diagonal(gram_total) / total - mean * mean
    scale = lax.rsqrt(variance + EPS)
    sums_total = jnp.sum(sums, axis=0)
    cross_total = jnp.sum(cross, axis=0)
    trait_total = jnp.sum(trait_sums, axis=0)
    ratios = jnp.array(RATIOS, dtype=jnp.float32)
    identity = jnp.eye(width, dtype=jnp.float32)

    def train_system(fold):
        train_gram = gram_total - lax.dynamic_index_in_dim(gram, fold, 0, keepdims=False)
        train_sums = sums_total - lax.dynamic_index_in_dim(sums, fold, 0, keepdims=False)
        train_count = total - lax.dynamic_index_in_dim(counts, fold, 0, keepdims=False)
        train_cross = cross_total - lax.dynamic_index_in_dim(cross, fold, 0, keepdims=False)
        train_traits = trait_total - lax.dynamic_index_in_dim(trait_sums, fold, 0, keepdims=False)
        centered = (
            train_gram
            - mean[:, None] * train_sums[None, :]
            - train_sums[:, None] * mean[None, :]
            + train_count * mean[:, None] * mean[None, :]
        )
        system = scale[:, None] * centered * scale[None, :]
        target = scale[:, None] * (train_cross.T - mean[:, None] * train_traits[None, :])
        return (system, target)

    systems_count = FOLDS * SHRINK
    samp_size = lax.axis_size(SAMP)
    per_device = -(-systems_count // samp_size)
    first = lax.axis_index(SAMP) * per_device

    def solve_own(offset):
        which = jnp.minimum(first + offset, systems_count - 1)
        fold = which // SHRINK
        shrink = which - fold * SHRINK
        system, target = train_system(fold)
        penalty = jnp.sum(
            jnp.where(jnp.arange(SHRINK, dtype=jnp.int32) == shrink, ratios * width, 0.0)
        )
        beta = solve_batch((system + penalty * identity)[None], target[None])[0]
        return (scale[:, None] * beta).astype(jnp.bfloat16)

    owned = lax.map(solve_own, jnp.arange(per_device, dtype=jnp.int32))
    collected = lax.all_gather(owned, SAMP, axis=0, tiled=True)
    coef = collected[:systems_count].reshape(FOLDS, SHRINK, width, traits_count)
    coef_flat = coef.transpose(2, 0, 1, 3).reshape(width, FOLDS * SHRINK * traits_count)
    shift = jnp.einsum("v,klvt->klt", mean, coef.astype(jnp.float32), precision=HIGH)
    raw = jnp.einsum("vc,rv->cr", coef_flat, dosages, preferred_element_type=jnp.float32)
    outcome = raw.reshape(FOLDS, SHRINK, traits_count, rows) - shift[..., None]
    level_pred = jnp.einsum("kltr,kr->ltr", outcome, masks, precision=HIGH)
    group = traits_count // lax.axis_size("blk")
    start = lax.axis_index("blk") * group
    own_traits = lax.dynamic_slice_in_dim(traits_wide, start, group, 0)
    own_sums = lax.dynamic_slice_in_dim(trait_sums, start, group, 1)
    arrived = lax.all_to_all(level_pred[None], "blk", split_axis=2, concat_axis=0, tiled=True)
    count_pred = arrived.shape[0] * arrived.shape[1]
    flat = arrived.reshape(count_pred, group, rows)
    raw_grams = jnp.einsum("ks,ats,bts->ktab", masks, flat, flat, precision=HIGH)
    raw_sums = jnp.einsum("ks,ats->kta", masks, flat, precision=HIGH)
    raw_cross = jnp.einsum("ks,ats,ts->kta", masks, flat, own_traits, precision=HIGH)
    packed = jnp.concatenate(
        [
            raw_grams.reshape(FOLDS * group, count_pred * count_pred),
            raw_sums.reshape(FOLDS * group, count_pred),
            raw_cross.reshape(FOLDS * group, count_pred),
        ],
        axis=1,
    )
    packed = psum_tree(packed)
    raw_grams = packed[:, : count_pred * count_pred].reshape(FOLDS, group, count_pred, count_pred)
    raw_sums = packed[:, count_pred * count_pred : count_pred * (count_pred + 1)].reshape(
        FOLDS, group, count_pred
    )
    raw_cross = packed[:, count_pred * (count_pred + 1) :].reshape(FOLDS, group, count_pred)
    pred_sum = jnp.sum(raw_sums, axis=0)
    pred_sq = jnp.sum(jnp.diagonal(raw_grams, axis1=2, axis2=3), axis=0)
    pred_mean = pred_sum / total
    pred_var = pred_sq / total - pred_mean * pred_mean
    pred_scale = lax.rsqrt(pred_var + EPS)
    level0 = (flat - pred_mean.T[:, :, None]) * pred_scale.T[:, :, None]
    fold_mean = pred_mean[None]
    fold_sums = (raw_sums - counts[:, None, None] * fold_mean) * pred_scale[None]
    fold_grams = (
        raw_grams
        - fold_mean[..., :, None] * raw_sums[..., None, :]
        - raw_sums[..., :, None] * fold_mean[..., None, :]
        + counts[:, None, None, None] * fold_mean[..., :, None] * fold_mean[..., None, :]
    ) * (pred_scale[None, :, :, None] * pred_scale[None, :, None, :])
    fold_cross = (raw_cross - fold_mean * own_sums[:, :, None]) * pred_scale[None]
    level0 = level0.reshape(arrived.shape)
    train_grams = jnp.sum(fold_grams, axis=0)[None] - fold_grams
    train_cross = jnp.sum(fold_cross, axis=0)[None] - fold_cross
    shrunk = train_grams + total / 4.0 * jnp.eye(count_pred, dtype=jnp.float32)
    weights = solve_batch(
        shrunk.reshape(-1, count_pred, count_pred), train_cross.reshape(-1, count_pred)
    )
    weights = weights.reshape(FOLDS, group, count_pred)
    every_fold = jnp.einsum("ats,kta->kts", level0.reshape(flat.shape), weights, precision=HIGH)
    blended = jnp.einsum("kts,ks->ts", every_fold, masks, precision=HIGH)
    blend_sum = jnp.einsum("kta,kta->t", weights, fold_sums, precision=HIGH)
    blend_sq = jnp.einsum("kta,ktab,ktb->t", weights, fold_grams, weights, precision=HIGH)
    blend_mean = blend_sum / total
    blend_var = blend_sq / total - blend_mean * blend_mean
    blend = (blended - blend_mean[:, None]) * lax.rsqrt(blend_var + EPS)[:, None]
    return (level0, blend)


def view_of(mesh):
    devices = np.asarray(mesh.devices)
    samp, blk = devices.shape
    flat = list(devices.reshape(-1))
    xs = sorted({d.coords[0] for d in flat})
    zs = sorted({d.coords[2] for d in flat})
    cores = samp // (len(xs) * len(zs))
    view = devices.reshape(len(xs), len(zs), cores, blk)
    for (i, j, c, b), d in np.ndenumerate(view):
        assert d.coords[0] == xs[i] and d.coords[2] == zs[j]
    return Mesh(view, ("x", "z", "c", "blk"))


def solution(mesh):
    view = view_of(mesh)
    in_specs = (P(SAMP, "blk"), P(None, SAMP), P(SAMP))
    out_specs = (P(None, None, "blk", SAMP), P("blk", SAMP))
    return jax.shard_map(shards, mesh=view, in_specs=in_specs, out_specs=out_specs, check_vma=False)
```

profile of v0, /device:TPU:8, one launch (start us, length us, event | category | flops | bytes accessed | tf_op | source)
XLA Modules:
  0.0 606.8 jit_solution(15835812869913055414)
XLA Ops:
  7.2 1.4 copy.176
  8.6 1.3 convert_bitcast_fusion
  9.9 0.9 pad_maximum_fusion
  10.8 5.5 fusion.2
  17.6 203.9 %all-reduce.3.cloned.1.call-done = f32[5,529,529]{1,2,0:T(8,128)} async-done(((f32[5,529,529]{1,2,0:T(8,128)}), f32[5,529,529]{1,2,0:T(8,128)}) %all-reduce.3.cloned.1.call-update) | async-done | bytes 5596836 | tf_op jit(solution)/shard_map/psum | solution.py:41
  221.5 1.5 slice_reduce_fusion.1
  223.5 0.9 fusion.108
  225.6 6.1 %fusion.109 = (f32[5,512,512]{1,2,0:T(8,128)}, f32[512,512]{0,1:T(8,128)S(1)}) fusion(f32[5,529,529]{1,2,0:T(8,128)} %all-reduce.3.cloned.1.call-done), kind=kLoop, calls=%fused_computation.227 | loop fusion | flops 1048576 | bytes 11534336 | tf_op jit(solution)/shard_map/slice | solution.py:42
  231.7 5.1 gather_fusion
  238.0 2.4 fusion.35
  240.9 11.7 %custom-call.57 = f32[1,128,128]{2,1,0:T(8,128)S(1)} custom-call(f32[1,128,128]{2,1,0:T(8,128)S(1)} %cholesky.302), custom_call_target="Cholesky" | custom-call | tf_op jit(solution)/shard_map/while/body/eval_jaxpr/jit(cholesky)/cholesky | solution.py:17
  252.8 9.8 %custom-call.58 = f32[1,1,128,128]{2,3,1,0:T(8,128)S(1)} custom-call(f32[1,1,128,128]{3,2,1,0:T(8,128)S(1)} %get-tuple-element.131), custom_call_target="InvertDiagBlocksLowerTriangular" | custom-call | tf_op jit(solution)/shard_map/while/body/eval_jaxpr/jit(cholesky)/cholesky | solution.py:17
  263.4 11.7 %custom-call.59 = f32[1,128,128]{2,1,0:T(8,128)S(1)} custom-call(f32[1,128,128]{2,1,0:T(8,128)S(1)} %cholesky.306), custom_call_target="Cholesky" | custom-call | tf_op jit(solution)/shard_map/while/body/eval_jaxpr/jit(cholesky)/cholesky | solution.py:17
  275.4 10.0 %custom-call.60 = f32[1,1,128,128]{2,3,1,0:T(8,128)S(1)} custom-call(f32[1,1,128,128]{3,2,1,0:T(8,128)S(1)} %get-tuple-element.129), custom_call_target="InvertDiagBlocksLowerTriangular" | custom-call | tf_op jit(solution)/shard_map/while/body/eval_jaxpr/jit(cholesky)/cholesky | solution.py:17
  286.3 11.7 %custom-call.61 = f32[1,128,128]{2,1,0:T(8,128)S(1)} custom-call(f32[1,128,128]{2,1,0:T(8,128)S(1)} %cholesky.311), custom_call_target="Cholesky" | custom-call | tf_op jit(solution)/shard_map/while/body/eval_jaxpr/jit(cholesky)/cholesky | solution.py:17
  298.2 9.8 %custom-call.62 = f32[1,1,128,128]{2,3,1,0:T(8,128)S(1)} custom-call(f32[1,1,128,128]{3,2,1,0:T(8,128)S(1)} %get-tuple-element.127), custom_call_target="InvertDiagBlocksLowerTriangular" | custom-call | tf_op jit(solution)/shard_map/while/body/eval_jaxpr/jit(cholesky)/cholesky | solution.py:17
  308.8 11.9 %custom-call.63 = f32[1,128,128]{2,1,0:T(8,128)S(1)} custom-call(f32[1,128,128]{2,1,0:T(8,128)S(1)} %fusion.21), custom_call_target="Cholesky" | custom-call | tf_op jit(solution)/shard_map/while/body/eval_jaxpr/jit(cholesky)/cholesky | solution.py:17
  320.8 0.6 compare_reduce_fusion.2
  321.5 0.7 compare_reduce_fusion.1
  322.1 0.7 compare_reduce_fusion.3
  325.5 8.1 %while.1 = (s32[]{:T(128)}, f32[1,512,512]{1,2,0:T(8,128)S(1)}, s32[4,2]{0,1:T(2,128)S(1)}, f32[4,1,128,128]{3,2,1,0:T(8,128)S(1)}, s32[]{:T(128)}) while((s32[]{:T(128)}, f32[1,512,512]{1,2,0:T(8,128)S(1)}, s32[4,2]{0,1:T(2,128)S(1)}, f32[4,1,128,128]{3,2,1,0:T(8,128)S(1)}, s32[]{:T(128)}) %tuple.57), condition=%wide.while_cond, body=%wide.while_body.sunk | while | flops 2 | bytes 393333 | solution.py:20
  326.1 1.3 constant_dynamic-slice_fusion.11
  328.2 1.3 constant_dynamic-slice_fusion.11
  330.2 1.3 constant_dynamic-slice_fusion.11
  332.2 1.3 constant_dynamic-slice_fusion.11
  333.7 39.3 %custom-call.64 = f32[1,4,128,128]{2,3,1,0:T(8,128)S(1)} custom-call(f32[1,4,128,128]{3,2,1,0:T(8,128)S(1)} %bitcast.370), custom_call_target="InvertDiagBlocksLowerTriangular" | custom-call | tf_op jit(solution)/shard_map/while/body/eval_jaxpr/vmap(jit(_cho_solve))/triangular_solve | solution.py:20
  373.0 1.8 fusion.107
  374.8 0.7 copy.187
  375.7 0.8 fusion.106
  376.5 0.8 fusion.72
  380.3 0.7 fusion.70
  381.0 0.7 dynamic-slice_convert_fusion
  382.4 74.5 %all-gather.2.cloned.1.call-done = bf16[64,512,16]{1,2,0:T(8,128)(2,1)} async-done(((bf16[1,512,16]{1,2,0:T(8,128)(2,1)}), bf16[64,512,16]{1,2,0:T(8,128)(2,1)}) %all-gather.2.cloned.1.call-update) | async-done | bytes 1048592 | tf_op jit(solution)/shard_map/all_gather | solution.py:91
  456.8 1.0 slice.263
  457.9 1.5 fusion.111
  459.9 0.9 copy.188
  460.8 4.8 all-to-all-start
  466.2 4.4 all-to-all-done
  471.8 1.3 fusion.13
  473.4 3.5 psum.29
  476.9 29.2 %psum.30 = f32[20,440]{1,0:T(8,128)S(1)} all-reduce(f32[20,440]{1,0:T(8,128)S(1)} %psum.29), channel_id=1, replica_groups=mesh['x'=4,'z'=8,'c'=2,'blk'=4] {'z'}, use_global_device_ids=true, to_apply=%region_16.17 | all-reduce | flops 8800 | bytes 70400 | tf_op jit(solution)/shard_map/psum | solution.py:27
  506.1 16.2 %psum.31 = f32[20,440]{1,0:T(8,128)S(1)} all-reduce(f32[20,440]{1,0:T(8,128)S(1)} %psum.30), channel_id=1, replica_groups=mesh['x'=4,'z'=8,'c'=2,'blk'=4] {'x'}, use_global_device_ids=true, to_apply=%region_17.18 | all-reduce | flops 8800 | bytes 70400 | tf_op jit(solution)/shard_map/psum | solution.py:27
  523.2 0.8 gather_fusion.1
  527.4 36.7 %custom-call.65 = f32[20,20,20]{2,1,0:T(8,128)S(1)} custom-call(f32[20,20,20]{2,1,0:T(8,128)S(1)} %fusion.44), custom_call_target="Cholesky" | custom-call | tf_op jit(solution)/shard_map/jit(cholesky)/cholesky | solution.py:17
  564.4 30.9 %custom-call.66 = f32[20,1,20,20]{2,3,1,0:T(8,128)S(1)} custom-call(f32[20,1,20,20]{3,2,1,0:T(8,128)S(1)} %select_bitcast_fusion), custom_call_target="InvertDiagBlocksLowerTriangular" | custom-call | tf_op jit(solution)/shard_map/vmap(jit(_cho_solve))/triangular_solve | solution.py:20
  596.6 0.7 copy.213
  598.4 0.6 add_rsqrt_fusion.2
  599.0 0.7 multiply_bitcast_fusion.1
  (156 shorter events, 22.0 us)
Async XLA Ops:
  7.2 214.3 %all-reduce.3.cloned.1.call-start = ((), (), s32[]{:S(2)}) async-start(), calls=%async_computation.1 | async-start | bytes 13721600 | tf_op jit(solution)/shard_map/psum | solution.py:41
  16.3 0.7 copy-start.4
  16.4 440.5 %all-gather.2.cloned.1.call-start = ((), (), s32[]{:S(2)}) async-start(), calls=%async_computation.2 | async-start | bytes 1064960 | tf_op jit(solution)/shard_map/all_gather | solution.py:91
  373.0 86.4 %copy-start = (bf16[640,512]{1,0:T(8,128)(2,1)S(1)}, bf16[640,512]{1,0:T(8,128)(2,1)}, u32[]{:S(2)}) copy-start(bf16[640,512]{1,0:T(8,128)(2,1)} %param.4) | copy-start | bytes 1966084
  375.6 83.8 %copy-start.1 = (f32[640,5]{0,1:T(8,128)S(1)}, f32[640,5]{0,1:T(8,128)}, u32[]{:S(2)}) copy-start(f32[640,5]{0,1:T(8,128)} %get-tuple-element.137) | copy-start | bytes 38404
  378.1 92.7 %copy-start.2 = (s32[640]{0:T(1024)S(1)}, s32[640]{0:T(1024)}, u32[]{:S(2)}) copy-start(s32[640]{0:T(1024)} %param.6) | copy-start | bytes 7684
  380.1 91.7 %copy-start.3 = (f32[640,5]{0,1:T(8,128)S(1)}, f32[640,5]{0,1:T(8,128)}, u32[]{:S(2)}) copy-start(f32[640,5]{0,1:T(8,128)} %get-tuple-element.136) | copy-start | bytes 38404
  460.8 9.8 %all-to-all-start = ((f32[1,5,16,640]{3,0,1,2:T(1,128)}), f32[1,5,16,640]{3,0,1,2:T(1,128)S(1)}, u32[]{:S(2)}, u32[]{:S(2)}) async-start(f32[1,5,16,640]{3,0,1,2:T(1,128)} %copy.188), calls=%async_computation | async-start | bytes 409600 | tf_op jit(solution)/shard_map/all_to_all | solution.py:102
Sparse Core Ops, SparseCore 0:
  16.5 204.9 all-reduce.2
  381.1 75.6 all-gather.1
where the time goes:
time: 611 us; the launch traced here: 607 us
  waiting for transfers between devices  283 us (46%)
  other arithmetic  210 us (34%)
  blocking collectives  48.9 us (8%)
  local copies, waits for them, and re-layouts  24 us (4%)
  between operations  19.3 us (3%)
  matrix products  16.7 us (3%)
    psum x1, waiting for transfers between devices, shards(): stats = lax.psum(stats, SAMP)  204 us
    another operation x18, other arithmetic, solve_batch(): factors = jnp.linalg.cholesky(systems)  116 us
    all_gather x1, waiting for transfers between devices, shards(): collected = lax.all_gather(owned, SAMP, axis=0, tiled=True)  74.5 us
    another operation x6, other arithmetic, solve_single(): return jax.scipy.linalg.cho_solve((factor, True), right_side)  70.5 us
    psum x3, blocking collectives, psum_tree(): value = lax.psum(value, name)  48.9 us
  transfers between devices with their start and end apart: 3, of which 3 were waited for; matrix products, arithmetic and copies ran while one was open for 0% of the time, Pallas kernels for 0%

commit v1 on v0

--- a/solution.py
+++ b/solution.py
@@ -88,7 +88,9 @@
         return (scale[:, None] * beta).astype(jnp.bfloat16)
 
     owned = lax.map(solve_own, jnp.arange(per_device, dtype=jnp.int32))
-    collected = lax.all_gather(owned, SAMP, axis=0, tiled=True)
+    f_next = jnp.stack([owned for _ in range(lax.axis_size(SAMP))])
+    last = lax.all_to_all(f_next, SAMP, 0, 0)
+    collected = jnp.concatenate(last, axis=0)
     coef = collected[:systems_count].reshape(FOLDS, SHRINK, width, traits_count)
     coef_flat = coef.transpose(2, 0, 1, 3).reshape(width, FOLDS * SHRINK * traits_count)
     shift = jnp.einsum("v,klvt->klt", mean, coef.astype(jnp.float32), precision=HIGH)

time: 611 us -> 573 us (0.938)
  waiting for transfers between devices: 283 us -> 235 us
  starting transfers between devices: 4.9 us -> 13 us
    all_gather x1 -> x0, waiting for transfers between devices: 74.5 us -> none  [shards(): collected = lax.all_gather(owned, SAMP, axis=0, tiled=True)]
    all_to_all x0 -> x1, waiting for transfers between devices: none -> 26.8 us  [shards(): last = lax.all_to_all(f_next, SAMP, 0, 0)]
    all_to_all x0 -> x1, starting transfers between devices: none -> 8.14 us  [shards(): last = lax.all_to_all(f_next, SAMP, 0, 0)]
where the time goes in v1:
time: 573 us; the launch traced here: 568 us
  waiting for transfers between devices  235 us (41%)
  other arithmetic  209 us (36%)
  blocking collectives  49.3 us (9%)
  local copies, waits for them, and re-layouts  26 us (5%)
  between operations  19.3 us (3%)
  matrix products  16.7 us (3%)
  starting transfers between devices  13 us (2%)
    psum x1, waiting for transfers between devices, shards(): stats = lax.psum(stats, SAMP)  204 us
    another operation x18, other arithmetic, solve_batch(): factors = jnp.linalg.cholesky(systems)  116 us
    another operation x6, other arithmetic, solve_single(): return jax.scipy.linalg.cho_solve((factor, True), right_side)  71.3 us
    psum x3, blocking collectives, psum_tree(): value = lax.psum(value, name)  49.3 us
    all_to_all x1, waiting for transfers between devices, shards(): last = lax.all_to_all(f_next, SAMP, 0, 0)  26.8 us
  transfers between devices with their start and end apart: 3, of which 3 were waited for; matrix products, arithmetic and copies ran while one was open for 0% of the time, Pallas kernels for 0%

profile of v1, /device:TPU:8, one launch (start us, length us, event | category | flops | bytes accessed | tf_op | source)
XLA Modules:
  0.0 568.5 jit_solution(6021007631954418304)
XLA Ops:
  7.2 1.4 copy.177
  8.6 0.7 convert_bitcast_fusion
  9.3 0.9 pad_maximum_fusion
  10.2 5.5 fusion.2
  17.0 203.9 %all-reduce.3.cloned.1.call-done = f32[5,529,529]{1,2,0:T(8,128)} async-done(((f32[5,529,529]{1,2,0:T(8,128)}), f32[5,529,529]{1,2,0:T(8,128)}) %all-reduce.3.cloned.1.call-update) | async-done | bytes 5596836 | tf_op jit(solution)/shard_map/psum | solution.py:41
  220.9 1.5 slice_reduce_fusion.1
  222.9 0.9 fusion.113
  225.0 6.1 %fusion.114 = (f32[5,512,512]{1,2,0:T(8,128)}, f32[512,512]{0,1:T(8,128)S(1)}) fusion(f32[5,529,529]{1,2,0:T(8,128)} %all-reduce.3.cloned.1.call-done), kind=kLoop, calls=%fused_computation.229 | loop fusion | flops 1048576 | bytes 11534336 | tf_op jit(solution)/shard_map/slice | solution.py:42
  231.1 5.1 gather_fusion
  237.4 2.4 fusion.35
  240.3 11.7 %custom-call.57 = f32[1,128,128]{2,1,0:T(8,128)S(1)} custom-call(f32[1,128,128]{2,1,0:T(8,128)S(1)} %cholesky.302), custom_call_target="Cholesky" | custom-call | tf_op jit(solution)/shard_map/while/body/eval_jaxpr/jit(cholesky)/cholesky | solution.py:17
  252.2 9.8 %custom-call.58 = f32[1,1,128,128]{2,3,1,0:T(8,128)S(1)} custom-call(f32[1,1,128,128]{3,2,1,0:T(8,128)S(1)} %get-tuple-element.131), custom_call_target="InvertDiagBlocksLowerTriangular" | custom-call | tf_op jit(solution)/shard_map/while/body/eval_jaxpr/jit(cholesky)/cholesky | solution.py:17
  262.8 11.7 %custom-call.59 = f32[1,128,128]{2,1,0:T(8,128)S(1)} custom-call(f32[1,128,128]{2,1,0:T(8,128)S(1)} %cholesky.306), custom_call_target="Cholesky" | custom-call | tf_op jit(solution)/shard_map/while/body/eval_jaxpr/jit(cholesky)/cholesky | solution.py:17
  274.8 10.0 %custom-call.60 = f32[1,1,128,128]{2,3,1,0:T(8,128)S(1)} custom-call(f32[1,1,128,128]{3,2,1,0:T(8,128)S(1)} %get-tuple-element.129), custom_call_target="InvertDiagBlocksLowerTriangular" | custom-call | tf_op jit(solution)/shard_map/while/body/eval_jaxpr/jit(cholesky)/cholesky | solution.py:17
  285.7 11.7 %custom-call.61 = f32[1,128,128]{2,1,0:T(8,128)S(1)} custom-call(f32[1,128,128]{2,1,0:T(8,128)S(1)} %cholesky.311), custom_call_target="Cholesky" | custom-call | tf_op jit(solution)/shard_map/while/body/eval_jaxpr/jit(cholesky)/cholesky | solution.py:17
  297.6 9.8 %custom-call.62 = f32[1,1,128,128]{2,3,1,0:T(8,128)S(1)} custom-call(f32[1,1,128,128]{3,2,1,0:T(8,128)S(1)} %get-tuple-element.127), custom_call_target="InvertDiagBlocksLowerTriangular" | custom-call | tf_op jit(solution)/shard_map/while/body/eval_jaxpr/jit(cholesky)/cholesky | solution.py:17
  308.2 11.9 %custom-call.63 = f32[1,128,128]{2,1,0:T(8,128)S(1)} custom-call(f32[1,128,128]{2,1,0:T(8,128)S(1)} %fusion.21), custom_call_target="Cholesky" | custom-call | tf_op jit(solution)/shard_map/while/body/eval_jaxpr/jit(cholesky)/cholesky | solution.py:17
  320.2 0.6 compare_reduce_fusion.2
  320.9 0.7 compare_reduce_fusion.1
  321.5 0.7 compare_reduce_fusion.3
  324.9 10.5 %while.1 = (s32[]{:T(128)}, f32[1,512,512]{1,2,0:T(8,128)S(1)}, s32[4,2]{0,1:T(2,128)S(1)}, f32[4,1,128,128]{3,2,1,0:T(8,128)}, s32[]{:T(128)}) while((s32[]{:T(128)}, f32[1,512,512]{1,2,0:T(8,128)S(1)}, s32[4,2]{0,1:T(2,128)S(1)}, f32[4,1,128,128]{3,2,1,0:T(8,128)}, s32[]{:T(128)}) %tuple.57), condition=%wide.while_cond, body=%wide.while_body.sunk | while | flops 2 | bytes 393333 | solution.py:20
  325.5 1.3 constant_dynamic-slice_fusion.11
  326.9 0.6 bitcast_dynamic-update-slice_fusion.2
  328.2 1.3 constant_dynamic-slice_fusion.11
  330.8 1.3 constant_dynamic-slice_fusion.11
  332.2 0.6 bitcast_dynamic-update-slice_fusion.2
  333.4 1.3 constant_dynamic-slice_fusion.11
  334.8 0.6 bitcast_dynamic-update-slice_fusion.2
  335.4 40.1 %custom-call.64 = f32[1,4,128,128]{2,3,1,0:T(8,128)S(1)} custom-call(f32[1,4,128,128]{3,2,1,0:T(8,128)} %bitcast.371), custom_call_target="InvertDiagBlocksLowerTriangular" | custom-call | tf_op jit(solution)/shard_map/while/body/eval_jaxpr/vmap(jit(_cho_solve))/triangular_solve | solution.py:20
  375.6 1.8 fusion.112
  377.6 0.9 fusion.111
  381.6 1.1 stack.2
  382.7 8.1 %all-to-all-start = ((bf16[64,1,512,16]{2,3,1,0:T(8,128)(2,1)}), bf16[64,1,512,16]{2,3,1,0:T(8,128)(2,1)S(1)}, u32[]{:S(2)}, u32[]{:S(2)}) async-start(bf16[64,1,512,16]{2,3,1,0:T(8,128)(2,1)} %stack.2), calls=%async_computation | async-start | bytes 2097152 | tf_op jit(solution)/shard_map/all_to_all | solution.py:92
  390.9 0.7 dynamic-slice_convert_fusion
  392.2 26.8 %all-to-all-done = bf16[64,1,512,16]{2,3,1,0:T(8,128)(2,1)S(1)} async-done(((bf16[64,1,512,16]{2,3,1,0:T(8,128)(2,1)}), bf16[64,1,512,16]{2,3,1,0:T(8,128)(2,1)S(1)}, u32[]{:S(2)}, u32[]{:S(2)}) %all-to-all-start) | async-done | bytes 1048608 | tf_op jit(solution)/shard_map/all_to_all | solution.py:92
  419.0 1.5 fusion.40
  421.0 0.9 copy.189
  421.9 4.8 all-to-all-start.1
  427.4 4.6 all-to-all-done.1
  433.2 1.3 fusion.13
  434.8 3.5 psum.29
  438.3 28.6 %psum.30 = f32[20,440]{1,0:T(8,128)S(1)} all-reduce(f32[20,440]{1,0:T(8,128)S(1)} %psum.29), channel_id=1, replica_groups=mesh['x'=4,'z'=8,'c'=2,'blk'=4] {'z'}, use_global_device_ids=true, to_apply=%region_16.17 | all-reduce | flops 8800 | bytes 70400 | tf_op jit(solution)/shard_map/psum | solution.py:27
  466.9 17.1 %psum.31 = f32[20,440]{1,0:T(8,128)S(1)} all-reduce(f32[20,440]{1,0:T(8,128)S(1)} %psum.30), channel_id=1, replica_groups=mesh['x'=4,'z'=8,'c'=2,'blk'=4] {'x'}, use_global_device_ids=true, to_apply=%region_17.18 | all-reduce | flops 8800 | bytes 70400 | tf_op jit(solution)/shard_map/psum | solution.py:27
  484.9 0.8 gather_fusion.1
  489.1 36.7 %custom-call.65 = f32[20,20,20]{2,1,0:T(8,128)S(1)} custom-call(f32[20,20,20]{2,1,0:T(8,128)S(1)} %fusion.46), custom_call_target="Cholesky" | custom-call | tf_op jit(solution)/shard_map/jit(cholesky)/cholesky | solution.py:17
  526.0 30.9 %custom-call.66 = f32[20,1,20,20]{2,3,1,0:T(8,128)S(1)} custom-call(f32[20,1,20,20]{3,2,1,0:T(8,128)S(1)} %select_bitcast_fusion), custom_call_target="InvertDiagBlocksLowerTriangular" | custom-call | tf_op jit(solution)/shard_map/vmap(jit(_cho_solve))/triangular_solve | solution.py:20
  558.3 0.7 copy.214
  560.7 0.7 multiply_bitcast_fusion.1
  (152 shorter events, 23.5 us)
Async XLA Ops:
  7.2 213.7 %all-reduce.3.cloned.1.call-start = ((), (), s32[]{:S(2)}) async-start(), calls=%async_computation.2 | async-start | bytes 13721600 | tf_op jit(solution)/shard_map/psum | solution.py:41
  15.7 0.7 copy-start.2
  377.5 43.0 %copy-start = (bf16[640,512]{1,0:T(8,128)(2,1)S(1)}, bf16[640,512]{1,0:T(8,128)(2,1)}, u32[]{:S(2)}) copy-start(bf16[640,512]{1,0:T(8,128)(2,1)} %param.4) | copy-start | bytes 1966084
  382.7 49.5 %copy-start.1 = (s32[640]{0:T(1024)S(1)}, s32[640]{0:T(1024)}, u32[]{:S(2)}) copy-start(s32[640]{0:T(1024)} %param.6) | copy-start | bytes 7684
  382.7 36.3 %all-to-all-start = ((bf16[64,1,512,16]{2,3,1,0:T(8,128)(2,1)}), bf16[64,1,512,16]{2,3,1,0:T(8,128)(2,1)S(1)}, u32[]{:S(2)}, u32[]{:S(2)}) async-start(bf16[64,1,512,16]{2,3,1,0:T(8,128)(2,1)} %stack.2), calls=%async_computation | async-start | bytes 2097152 | tf_op jit(solution)/shard_map/all_to_all | solution.py:92
  421.9 10.0 %all-to-all-start.1 = ((f32[1,5,16,640]{3,0,1,2:T(1,128)}), f32[1,5,16,640]{3,0,1,2:T(1,128)S(1)}, u32[]{:S(2)}, u32[]{:S(2)}) async-start(f32[1,5,16,640]{3,0,1,2:T(1,128)} %copy.189), calls=%async_computation.1 | async-start | bytes 409600 | tf_op jit(solution)/shard_map/all_to_all | solution.py:104
Sparse Core Ops, SparseCore 0:
  15.9 204.9 all-reduce.2
